TPU v7x, 32 devices: a whole 2x2x4 slice. The times are simulated.
32 devices in a mesh: dp: 8 (over z, y), tensor: 4 (over x, core).
Axes of the slice: x: 2, y: 2, z: 4, core: 2. Of those that a mesh axis runs over, the one named last changes fastest.
Arguments:
- pre_hidden: bfloat16 [8192, 2048], P(('dp', 'tensor')), may hold values from -6 to 6
- dec_hidden: bfloat16 [16, 2048], P('dp'), may hold values from -6 to 6
- norm_gain: bfloat16 [2048], replicated, may hold values from 0.5 to 1.5
- norm_shift: bfloat16 [2048], replicated, may hold values from -3 to 3
- qkv_weight: bfloat16 [2048, 6144], P(None, 'tensor'), may hold values from -0.125 to 0.125
- qkv_bias: bfloat16 [6144], P('tensor'), may hold values from -3 to 3
- out_weight: bfloat16 [2048, 2048], P('tensor'), may hold values from -0.125 to 0.125
- out_bias: bfloat16 [2048], replicated, may hold values from -3 to 3
- pre_keys: bfloat16 [8, 1024, 2048], P('dp', None, 'tensor'), may hold values from -480 to 480
- pre_values: bfloat16 [8, 1024, 2048], P('dp', None, 'tensor'), may hold values from -6 to 6
- dec_keys: bfloat16 [16, 2048, 2048], P('dp', None, 'tensor'), may hold values from -480 to 480
- dec_values: bfloat16 [16, 2048, 2048], P('dp', None, 'tensor'), may hold values from -6 to 6
- prefix_lengths: int32 [8], P('dp'), may hold values from 0 to 1024, as said below
- cache_lengths: int32 [16], P('dp'), may hold values from 1 to 2048, as said below
- slot_of: int32 [16], replicated, may hold values from 0 to 15, each once
Outputs:
- pre_output: bfloat16 [8192, 2048], P(('dp', 'tensor'))
- dec_output: bfloat16 [16, 2048], P('dp')
Inputs may be any that keep to these rules, and one draw needn't show every extreme that they name: `slot_of`: each decode slot is used by exactly one decode request. `prefix_lengths`: the longest prefix equals 1024. `cache_lengths`: the longest decode cache equals 2048.
All inputs are finite; a program needn't handle non-finite values.
Results may differ from a plain program's by a relative error of at most 0.0049.
The roundings to bfloat16 on the way count: a program that leaves them out, or rounds other values in their place, can miss the bound.
Values may be sent and summed in bfloat16 or wider, within the bound.
No kernel may reach another device: no remote copies, remote signals or barrier semaphores. Data moves between devices by JAX's collectives and lax.ppermute only.
A program may use at most 128 MiB of HBM per device.

v0:
```python
import math
import jax
import jax.numpy as jnp
from jax import lax
from jax.sharding import PartitionSpec as P

H = 16
HD = 128
EPSILON = 1e-05


def normalize(values, norm_gain, norm_shift):
    values = values.astype(jnp.float32)
    center = values - jnp.mean(values, axis=-1, keepdims=True)
    spread = jnp.mean(center * center, axis=-1, keepdims=True)
    scaled = center * lax.rsqrt(spread + EPSILON)
    return (scaled * norm_gain.astype(jnp.float32) + norm_shift.astype(jnp.float32)).astype(
        jnp.bfloat16
    )


def alibi_slopes(first_head, head_count, total_heads):
    head_ids = (first_head + jnp.arange(head_count, dtype=jnp.int32)).astype(jnp.float32)
    return jnp.exp2(-8.0 * (head_ids + 1.0) / total_heads)


def prefill_attention(merged_rows, cache_keys, cache_values, prefix, slopes):
    queries = merged_rows[:, :, 0]
    new_keys = merged_rows[:, :, 1]
    new_values = merged_rows[:, :, 2]
    group_size = merged_rows.shape[0]
    cache_size = cache_keys.shape[0]
    factor = 1.0 / math.sqrt(merged_rows.shape[-1])
    query_pos = prefix + jnp.arange(group_size, dtype=jnp.int32)
    cache_pos = jnp.arange(cache_size, dtype=jnp.int32)
    cache_dist = (query_pos[:, None] - cache_pos[None, :]).astype(jnp.float32)
    new_dist = (query_pos[:, None] - query_pos[None, :]).astype(jnp.float32)
    cache_scores = (
        jnp.einsum("qhd,khd->hqk", queries, cache_keys, preferred_element_type=jnp.float32) * factor
    )
    cache_scores = cache_scores - slopes[:, None, None] * cache_dist[None]
    cache_scores = jnp.where((cache_pos < prefix)[None, None, :], cache_scores, -jnp.inf)
    new_scores = (
        jnp.einsum("qhd,khd->hqk", queries, new_keys, preferred_element_type=jnp.float32) * factor
    )
    new_scores = new_scores - slopes[:, None, None] * new_dist[None]
    causal = (
        jnp.arange(group_size, dtype=jnp.int32)[None, :]
        <= jnp.arange(group_size, dtype=jnp.int32)[:, None]
    )
    new_scores = jnp.where(causal[None], new_scores, -jnp.inf)
    highest = jnp.maximum(
        jnp.max(cache_scores, axis=-1, keepdims=True), jnp.max(new_scores, axis=-1, keepdims=True)
    )
    cache_exp = jnp.exp(cache_scores - highest)
    new_exp = jnp.exp(new_scores - highest)
    denominator = jnp.sum(cache_exp, axis=-1, keepdims=True) + jnp.sum(
        new_exp, axis=-1, keepdims=True
    )
    cache_probs = (cache_exp / denominator).astype(jnp.bfloat16)
    new_probs = (new_exp / denominator).astype(jnp.bfloat16)
    context = jnp.einsum(
        "hqk,khd->qhd", cache_probs, cache_values, preferred_element_type=jnp.float32
    )
    context = context + jnp.einsum(
        "hqk,khd->qhd", new_probs, new_values, preferred_element_type=jnp.float32
    )
    return context.astype(jnp.bfloat16).reshape(group_size, -1)


def decode_attention(query_row, new_key, new_value, cache_keys, cache_values, length, slopes):
    factor = 1.0 / math.sqrt(query_row.shape[-1])
    cache_pos = jnp.arange(cache_keys.shape[0], dtype=jnp.int32)
    distance = (length - cache_pos).astype(jnp.float32)
    cache_scores = (
        jnp.einsum("hd,khd->hk", query_row, cache_keys, preferred_element_type=jnp.float32) * factor
    )
    cache_scores = cache_scores - slopes[:, None] * distance[None, :]
    cache_scores = jnp.where((cache_pos < length)[None, :], cache_scores, -jnp.inf)
    own_score = (
        jnp.einsum("hd,hd->h", query_row, new_key, preferred_element_type=jnp.float32)[:, None]
        * factor
    )
    highest = jnp.maximum(jnp.max(cache_scores, axis=-1, keepdims=True), own_score)
    cache_exp = jnp.exp(cache_scores - highest)
    own_exp = jnp.exp(own_score - highest)
    denominator = jnp.sum(cache_exp, axis=-1, keepdims=True) + own_exp
    cache_probs = (cache_exp / denominator).astype(jnp.bfloat16)
    own_prob = (own_exp / denominator).astype(jnp.bfloat16)
    context = jnp.einsum(
        "hk,khd->hd", cache_probs, cache_values, preferred_element_type=jnp.float32
    )
    context = context + own_prob.astype(jnp.float32) * new_value.astype(jnp.float32)
    return context.astype(jnp.bfloat16).reshape(-1)


def per_device(
    pre_hidden,
    dec_hidden,
    norm_gain,
    norm_shift,
    qkv_weight,
    qkv_bias,
    out_weight,
    out_bias,
    pre_keys,
    pre_values,
    dec_keys,
    dec_values,
    prefix_lengths,
    cache_lengths,
    slot_of,
):
    head_size = HD
    local_heads = qkv_weight.shape[1] // (3 * head_size)
    slopes = alibi_slopes(lax.axis_index("tensor") * local_heads, local_heads, H)
    bias_sum = out_bias.astype(jnp.float32)
    normed = normalize(pre_hidden, norm_gain, norm_shift)
    product = jnp.dot(
        lax.all_gather(normed, "tensor", axis=0, tiled=True),
        qkv_weight,
        preferred_element_type=jnp.float32,
    )
    merged_rows = (product + qkv_bias.astype(jnp.float32)).astype(jnp.bfloat16)
    group_size = merged_rows.shape[0]
    merged_rows = merged_rows.reshape(group_size, local_heads, 3, head_size)
    cache_size = pre_keys.shape[1]
    context = prefill_attention(
        merged_rows,
        pre_keys[0].reshape(cache_size, local_heads, head_size),
        pre_values[0].reshape(cache_size, local_heads, head_size),
        prefix_lengths[0],
        slopes,
    )
    summed = lax.psum_scatter(
        jnp.dot(context, out_weight, preferred_element_type=jnp.float32),
        "tensor",
        scatter_dimension=0,
        tiled=True,
    )
    pre_output = (summed + bias_sum + pre_hidden.astype(jnp.float32)).astype(jnp.bfloat16)
    slot_count = dec_hidden.shape[0]
    first_slot = lax.axis_index("dp") * slot_count
    slot_ids = first_slot + jnp.arange(slot_count, dtype=jnp.int32)
    request_ids = jnp.arange(slot_of.shape[0], dtype=jnp.int32)
    own_requests_slots = lax.dynamic_slice_in_dim(slot_of, first_slot, slot_count)
    to_slot = request_ids[:, None] == own_requests_slots[None, :]
    outgoing = jnp.zeros((slot_of.shape[0], dec_hidden.shape[1]), jnp.float32)
    for j in range(slot_count):
        outgoing = jnp.where(
            to_slot[:, j, None], dec_hidden[j][None, :].astype(jnp.float32), outgoing
        )
    arrived = lax.psum_scatter(outgoing, "dp", scatter_dimension=0, tiled=True).astype(jnp.bfloat16)
    normed_slots = normalize(arrived, norm_gain, norm_shift)
    merged_slots = (
        jnp.dot(normed_slots, qkv_weight, preferred_element_type=jnp.float32)
        + qkv_bias.astype(jnp.float32)
    ).astype(jnp.bfloat16)
    merged_slots = merged_slots.reshape(slot_count, local_heads, 3, head_size)
    dec_cache = dec_keys.shape[1]
    slot_context = jax.vmap(decode_attention, in_axes=(0, 0, 0, 0, 0, 0, None))(
        merged_slots[:, :, 0],
        merged_slots[:, :, 1],
        merged_slots[:, :, 2],
        dec_keys.reshape(slot_count, dec_cache, local_heads, head_size),
        dec_values.reshape(slot_count, dec_cache, local_heads, head_size),
        cache_lengths,
        slopes,
    )
    slot_partial = jnp.dot(slot_context, out_weight, preferred_element_type=jnp.float32)
    from_slot = slot_of[:, None] == slot_ids[None, :]
    returning = jnp.zeros((slot_of.shape[0], slot_partial.shape[1]), jnp.float32)
    for j in range(slot_count):
        returning = jnp.where(from_slot[:, j, None], slot_partial[j][None, :], returning)
    summed_all = lax.psum(returning, ("dp", "tensor"))
    slot_summed = lax.dynamic_slice_in_dim(summed_all, first_slot, slot_count)
    dec_output = (slot_summed + bias_sum + dec_hidden.astype(jnp.float32)).astype(jnp.bfloat16)
    return (pre_output, dec_output)


def solution(mesh):
    placed = (
        P(("dp", "tensor"), None),
        P("dp", None),
        P(),
        P(),
        P(None, "tensor"),
        P("tensor"),
        P("tensor", None),
        P(),
        P("dp", None, "tensor"),
        P("dp", None, "tensor"),
        P("dp", None, "tensor"),
        P("dp", None, "tensor"),
        P("dp"),
        P("dp"),
        P(),
    )
    return jax.shard_map(
        per_device,
        mesh=mesh,
        in_specs=placed,
        out_specs=(P(("dp", "tensor"), None), P("dp", None)),
        check_vma=False,
    )
```

profile of v0, /device:TPU:0, one launch (start us, length us, event | category | flops | bytes accessed | tf_op | source)
XLA Modules:
  0.0 232.2 jit_solution(11411439349456508695)
XLA Ops:
  8.1 0.8 convert_element_type.110
  8.9 0.7 convert_element_type.111
  9.6 1.4 convert_reduce_fusion
  11.1 1.6 fusion.10
  12.7 2.8 %fusion.13 = bf16[256,2048]{1,0:T(8,128)(2,1)} fusion(bf16[256,2048]{1,0:T(8,128)(2,1)} %param.15, f32[2048]{0:T(1024)S(1)} %convert_element_type.111, f32[2048]{0:T(1024)S(1)} %convert_element_type.110, f32[256]{0:T(256)S(1)} %add_rsqrt_fusion, f32[256]{0:T(256)S(1)} %broadcast_multiply_fusion), kind=kLoop, calls=%fused_computation.27 | loop fusion | flops 3145728 | bytes 2115584 | tf_op jit(solution)/shard_map/convert_element_type | solution.py:17
  15.8 40.1 %all-reduce.5 = bf16[16,2048]{1,0:T(8,128)(2,1)S(1)} all-reduce(f32[16,2048]{1,0:T(8,128)S(1)} %select_select_fusion.1), channel_id=3, replica_groups=mesh['dp'=8,'tensor'=4] {'dp'}, use_global_device_ids=true, to_apply=%region_7.8.clone | all-reduce | flops 32768 | bytes 196608
  56.0 0.6 dynamic-slice
  57.4 0.2 fusion.24
  57.6 3.8 %fusion.9 = bf16[2,1536]{1,0:T(2,128)(2,1)S(1)} fusion(bf16[2048,1536]{1,0:T(8,128)(2,1)} %param.19, bf16[2,2048]{1,0:T(2,128)(2,1)S(1)} %get-tuple-element.7, f32[2]{0:T(128)S(1)} %add_rsqrt_fusion.1, f32[2]{0:T(128)S(1)} %broadcast_multiply_fusion.1, f32[2048]{0:T(1024)S(1)} %convert_element_type.111, f32[2048]{0:T(1024)S(1)} %convert_element_type.110, ...), kind=kOutput, calls=%fused_computation.23 | convolution fusion | flops 12613632 | bytes 6328336 | tf_op jit(solution)/shard_map/dot_general | solution.py:156
  61.4 6.4 %copy.60 = bf16[2,2048,512]{1,2,0:T(8,128)(2,1)} copy(bf16[2,2048,512]{2,1,0:T(8,128)(2,1)} %param.25) | data formatting | bytes 8388608 | tf_op jit(solution)/shard_map/reshape | solution.py:165
  67.9 3.0 %fusion.34 = f32[2,4,1,2048]{3,2,1,0:T(1,128)S(1)} fusion(bf16[2,2048,4,128]{1,3,2,0:T(8,128)(2,1)} %bitcast.86, bf16[2,4,3,128]{3,2,1,0:T(4,128)(2,1)S(1)} %reshape.204), kind=kOutput, calls=%fused_computation.66 | convolution fusion | flops 4194304 | bytes 4263936 | tf_op jit(solution)/shard_map/vmap(hd,khd->hk)/dot_general | solution.py:76
  71.1 0.2 fusion.43
  71.3 0.2 fusion.20
  71.7 0.7 fusion.4
  72.4 0.4 fusion.37
  72.8 0.7 select_select_fusion
  73.6 1.3 iota_compare_fusion
  75.6 3.6 %subtract_convert_fusion = (f32[1024,1024]{0,1:T(8,128)}, f32[1024,1024]{0,1:T(8,128)}) fusion(s32[1024]{0:T(1024)S(1)} %iota_add_fusion), kind=kLoop, calls=%fused_computation.14 | loop fusion | flops 4194304 | bytes 8392704 | tf_op jit(solution)/shard_map/convert_element_type | solution.py:37
  79.1 1.3 reshape_squeeze.6
  80.5 2.3 copy.59
  82.8 11.2 %add_convert_fusion = bf16[1024,1536]{1,0:T(8,128)(2,1)} fusion(bf16[1024,2048]{1,0:T(8,128)(2,1)} %all-gather.2.cloned.1.call-done, bf16[2048,1536]{1,0:T(8,128)(2,1)} %param.19, f32[1536]{0:T(1024)S(1)} %convert_element_type.113), kind=kOutput, calls=%fused_computation.10 | convolution fusion | flops 6445596672 | bytes 13637632 | tf_op jit(solution)/shard_map/dot_general | solution.py:119
  94.0 4.7 %copy.40 = bf16[1024,1536]{0,1:T(8,128)(2,1)} copy(bf16[1024,1536]{1,0:T(8,128)(2,1)} %add_convert_fusion) | data formatting | bytes 6291456 | tf_op jit(solution)/shard_map/convert_element_type | solution.py:124
  98.7 10.9 %fusion.47 = (f32[4,1024]{1,0:T(4,128)S(1)}, f32[4,1024,1024]{1,2,0:T(8,128)}) fusion(f32[1024,1024]{0,1:T(8,128)} %get-tuple-element.15, f32[4]{0:T(128)S(1)} %multiply_exponential_fusion, bf16[1024,4,3,128]{0,3,2,1:T(8,128)(2,1)} %bitcast.87, pred[1024,1024]{0,1:T(8,128)(4,1)} %iota_compare_fusion), kind=kOutput, calls=%fused_computation.96 | convolution fusion | flops 1094709248 | bytes 24133648 | tf_op jit(solution)/shard_map/qhd,khd->hqk/dot_general | solution.py:44
  109.6 3.7 %fusion.46 = (f32[4,1024]{1,0:T(4,128)S(1)}, f32[4,1024,1024]{1,2,0:T(8,128)S(1)}) fusion(f32[1024,1024]{0,1:T(8,128)S(1)} %copy-done.1, f32[4]{0:T(128)S(1)} %multiply_exponential_fusion, bf16[1024,4,3,128]{0,3,2,1:T(8,128)(2,1)S(1)} %bitcast.88, bf16[1024,4,128]{2,1,0:T(4,128)(2,1)S(1)} %reshape_squeeze.6, pred[1024]{0:T(1024)(128)(4,1)S(1)} %iota_compare_fusion.2), kind=kOutput, calls=%fused_computation.95 | convolution fusion | flops 1094709248 | bytes 23086592 | tf_op jit(solution)/shard_map/qhd,khd->hqk/dot_general | solution.py:39
  113.3 8.4 %fusion.1 = (f32[4,1024]{1,0:T(4,128)S(1)}, f32[4,1024]{1,0:T(4,128)S(1)}) fusion(f32[4,1024,1024]{1,2,0:T(8,128)} %get-tuple-element.26, f32[4,1024]{1,0:T(4,128)S(1)} %max.12, f32[4,1024,1024]{1,2,0:T(8,128)S(1)} %get-tuple-element.24), kind=kLoop, calls=%fused_computation.7 | loop fusion | flops 16769024 | bytes 33603584 | tf_op jit(solution)/shard_map/reduce_sum | solution.py:57
  121.8 3.5 %fusion.2 = f32[4,1024,128]{1,2,0:T(8,128)S(1)} fusion(bf16[1024,4,128]{0,2,1:T(8,128)(2,1)S(1)} %bitcast.90, f32[4,1024,1024]{1,2,0:T(8,128)S(1)} %get-tuple-element.24, f32[4,1024]{1,0:T(4,128)S(1)} %add.158, f32[4,1024]{1,0:T(4,128)S(1)} %max.12), kind=kOutput, calls=%fused_computation.8 | convolution fusion | flops 1086324736 | bytes 19955712 | tf_op jit(solution)/shard_map/hqk,khd->qhd/dot_general | solution.py:62
  125.3 8.0 %fusion.15 = bf16[1024,4,128]{0,2,1:T(8,128)(2,1)S(1)} fusion(f32[4,1024,128]{1,2,0:T(8,128)S(1)} %fusion.2, f32[4,1024,1024]{1,2,0:T(8,128)} %get-tuple-element.26, f32[4,1024]{1,0:T(4,128)S(1)} %add.158, f32[4,1024]{1,0:T(4,128)S(1)} %max.12, bf16[1024,4,3,128]{0,3,2,1:T(8,128)(2,1)S(1)} %bitcast.89), kind=kOutput, calls=%fused_computation.30 | convolution fusion | flops 1087373312 | bytes 21004288 | tf_op jit(solution)/shard_map/hqk,khd->qhd/dot_general | solution.py:65
  133.2 5.6 %fusion.48 = f32[1024,2048]{1,0:T(8,128)} fusion(bf16[1024,512]{0,1:T(8,128)(2,1)S(1)} %bitcast.97, bf16[512,2048]{1,0:T(8,128)(2,1)S(1)} %copy-done), kind=kOutput, calls=%fused_computation.97 | convolution fusion | flops 2147483648 | bytes 11534336 | tf_op jit(solution)/shard_map/dot_general | solution.py:136
  138.9 0.7 copy-done.7
  139.5 80.9 %all-reduce.4.cloned.1.call-done = f32[16,2048]{1,0:T(8,128)} async-done(((f32[16,2048]{1,0:T(8,128)}), f32[16,2048]{1,0:T(8,128)}) %all-reduce.4.cloned.1.call-update) | async-done | bytes 131088 | tf_op jit(solution)/shard_map/psum | solution.py:175
  220.4 1.5 add_convert_fusion.1
  221.8 2.9 %fusion.14 = bf16[256,2048]{1,0:T(8,128)(2,1)} fusion(bf16[256,2048]{1,0:T(8,128)(2,1)S(1)} %copy-done.2, f32[256,2048]{1,0:T(8,128)} %reduce-scatter.2.cloned.1.call-done, f32[2048]{0:T(1024)S(1)} %convert_element_type.121), kind=kLoop, calls=%fused_computation.28 | loop fusion | flops 2097152 | bytes 4202496 | tf_op jit(solution)/shard_map/convert_element_type | solution.py:141
  (61 shorter events, 1.3 us)
Async XLA Ops:
  8.0 64.4 %copy-start = (bf16[512,2048]{1,0:T(8,128)(2,1)S(1)}, bf16[512,2048]{1,0:T(8,128)(2,1)}, u32[]{:S(2)}) copy-start(bf16[512,2048]{1,0:T(8,128)(2,1)} %param.21) | copy-start | bytes 6291460
  8.0 48.0 %copy-start.11 = (u32[32]{0:T(128)S(1)}, u32[32]{0:T(128)}, u32[]{:S(2)}) copy-start(u32[32]{0:T(128)} %constant.56) | copy-start | bytes 388
  8.0 7.5 %copy-start.10 = (s32[16]{0:T(128)S(1)}, s32[16]{0:T(128)}, u32[]{:S(2)}) copy-start(s32[16]{0:T(128)} %param.29) | copy-start | bytes 196
  8.0 7.7 %copy-start.5 = (bf16[2,2048]{1,0:T(2,128)(2,1)S(1)}, bf16[2,2048]{1,0:T(2,128)(2,1)}, u32[]{:S(2)}) copy-start(bf16[2,2048]{1,0:T(2,128)(2,1)} %param.16) | copy-start | bytes 24580
  8.0 47.9 %copy-start.6 = (bf16[1536]{0:T(1024)(128)(2,1)S(1)}, bf16[1536]{0:T(1024)(128)(2,1)}, u32[]{:S(2)}) copy-start(bf16[1536]{0:T(1024)(128)(2,1)} %param.20) | copy-start | bytes 9220
  8.1 74.7 %all-gather.2.cloned.1.call-start = ((), (), s32[]{:S(2)}) async-start(), calls=%async_computation.1 | async-start | bytes 5242880 | tf_op jit(solution)/shard_map/all_gather | solution.py:120
  15.5 204.9 %all-reduce.4.cloned.1.call-start = ((), (), s32[]{:S(2)}) async-start(), calls=%async_computation.3 | async-start | bytes 262144 | tf_op jit(solution)/shard_map/psum | solution.py:175
  67.8 3.1 %copy-start.8 = (s32[2]{0:T(128)S(1)}, s32[2]{0:T(128)}, u32[]{:S(2)}) copy-start(s32[2]{0:T(128)} %param.28) | copy-start | bytes 28
  67.8 3.9 %copy-start.9 = (bf16[2,2048,512]{2,1,0:T(8,128)(2,1)S(1)}, bf16[2,2048,512]{2,1,0:T(8,128)(2,1)}, u32[]{:S(2)}) copy-start(bf16[2,2048,512]{2,1,0:T(8,128)(2,1)} %param.26) | copy-start | bytes 12582916
  73.6 148.3 %reduce-scatter.2.cloned.1.call-start = ((), (), s32[]{:S(2)}) async-start(), calls=%async_computation.2 | async-start | bytes 10485760 | tf_op jit(solution)/shard_map/reduce_scatter | solution.py:135
  98.7 10.9 %copy-start.1 = (f32[1024,1024]{0,1:T(8,128)S(1)}, f32[1024,1024]{0,1:T(8,128)}, u32[]{:S(2)}) copy-start(f32[1024,1024]{0,1:T(8,128)} %get-tuple-element.16) | copy-start | bytes 12582916
  98.7 10.9 %copy-start.3 = (bf16[1024,1536]{0,1:T(8,128)(2,1)S(1)}, bf16[1024,1536]{0,1:T(8,128)(2,1)}, u32[]{:S(2)}) copy-start(bf16[1024,1536]{0,1:T(8,128)(2,1)} %copy.40) | copy-start | bytes 9437188
  113.3 8.5 %copy-start.4 = (bf16[1,1024,512]{1,2,0:T(8,128)(2,1)S(1)}, bf16[1,1024,512]{1,2,0:T(8,128)(2,1)}, u32[]{:S(2)}) copy-start(bf16[1,1024,512]{1,2,0:T(8,128)(2,1)} %copy.59) | copy-start | bytes 3145732
  138.8 0.7 copy-start.7
  138.8 83.0 %copy-start.2 = (bf16[256,2048]{1,0:T(8,128)(2,1)S(1)}, bf16[256,2048]{1,0:T(8,128)(2,1)}, u32[]{:S(2)}) copy-start(bf16[256,2048]{1,0:T(8,128)(2,1)} %param.15) | copy-start | bytes 3145732
Sparse Core Ops, SparseCore 0:
  15.6 37.1 all-gather.1
  139.0 69.1 reduce-scatter.1
Sparse Core Ops, SparseCore 1:
  73.6 146.7 all-reduce.3
where the time goes:
time: 233 us; the launch traced here: 232 us
  waiting for transfers between devices  80.9 us (35%)
  matrix products  50.6 us (22%)
  blocking collectives  40.1 us (17%)
  other arithmetic  27.2 us (12%)
  between operations  17.1 us (7%)
  local copies, waits for them, and re-layouts  16.2 us (7%)
    psum x1, waiting for transfers between devices, per_device(): summed_all = lax.psum(returning, ('dp', 'tensor'))  80.9 us
    unnamed x1, blocking collectives  40.1 us
    dot_general x1, matrix products, per_device(): jnp.dot(lax.all_gather(normed, 'tensor', axis=0, tiled=True), qkv_weight,...  11.2 us
    dot_general x1, matrix products, prefill_attention(): jnp.einsum('qhd,khd->hqk', queries, new_keys, preferred_element_type=jnp....  10.9 us
    reduce_sum x1, other arithmetic, prefill_attention(): jnp.sum(new_exp, axis=-1, keepdims=True)  8.43 us
    dot_general x1, matrix products, prefill_attention(): jnp.einsum('hqk,khd->qhd', new_probs, new_values, preferred_element_type=...  7.95 us
    reshape x1, local copies, waits for them, and re-layouts, per_device(): dec_keys.reshape(slot_count, dec_cache, local_heads, head_size)  6.41 us
    dot_general x1, matrix products, per_device(): jnp.dot(context, out_weight, preferred_element_type=jnp.float32)  5.61 us
  transfers between devices with their start and end apart: 3, of which 1 were waited for; matrix products, arithmetic and copies ran while one was open for 36% of the time, Pallas kernels for 0%

commit v1 on v0

--- a/solution.py
+++ b/solution.py
@@ -172,7 +172,7 @@
     returning = jnp.zeros((slot_of.shape[0], slot_partial.shape[1]), jnp.float32)
     for j in range(slot_count):
         returning = jnp.where(from_slot[:, j, None], slot_partial[j][None, :], returning)
-    summed_all = lax.psum(returning, ("dp", "tensor"))
+    summed_all = lax.psum(lax.psum(returning, "tensor"), "dp")
     slot_summed = lax.dynamic_slice_in_dim(summed_all, first_slot, slot_count)
     dec_output = (slot_summed + bias_sum + dec_hidden.astype(jnp.float32)).astype(jnp.bfloat16)
     return (pre_output, dec_output)

time: 233 us -> 295 us (1.27)
  waiting for transfers between devices: 80.9 us -> 139 us
  matrix products: 50.6 us -> 54.7 us
    reduce_scatter x1, waiting for transfers between devices: 0.01 us -> 72 us  [per_device(): lax.psum_scatter(jnp.dot(context, out_weight, preferred_element_type=jnp....]
    psum x1 -> x2, waiting for transfers between devices: 80.9 us -> 31 us  [per_device(): summed_all = lax.psum(lax.psum(returning, 'tensor'), 'dp')]
    all_gather x1, waiting for transfers between devices: 0.01 us -> 35.9 us  [per_device(): lax.all_gather(normed, 'tensor', axis=0, tiled=True)]
  transfers between devices with their start and end apart: 3 -> 4, of which waited for: 1 -> 4; matrix products, arithmetic and copies ran while one was open for 36% -> 24% of each run, Pallas kernels for 0% -> 0%
where the time goes in v1:
time: 295 us; the launch traced here: 294 us
  waiting for transfers between devices  139 us (47%)
  matrix products  54.7 us (19%)
  blocking collectives  40.2 us (14%)
  other arithmetic  26.4 us (9%)
  local copies, waits for them, and re-layouts  18.1 us (6%)
  between operations  15.3 us (5%)
    reduce_scatter x1, waiting for transfers between devices, per_device(): lax.psum_scatter(jnp.dot(context, out_weight, preferred_element_type=jnp....  72 us
    unnamed x1, blocking collectives  40.2 us
    all_gather x1, waiting for transfers between devices, per_device(): lax.all_gather(normed, 'tensor', axis=0, tiled=True)  35.9 us
    psum x2, waiting for transfers between devices, per_device(): summed_all = lax.psum(lax.psum(returning, 'tensor'), 'dp')  31 us
    dot_general x1, matrix products, per_device(): jnp.dot(lax.all_gather(normed, 'tensor', axis=0, tiled=True), qkv_weight,...  11.2 us
    dot_general x1, matrix products, prefill_attention(): jnp.einsum('qhd,khd->hqk', queries, new_keys, preferred_element_type=jnp....  10.9 us
    reduce_sum x1, other arithmetic, prefill_attention(): jnp.sum(new_exp, axis=-1, keepdims=True)  8.44 us
    dot_general x1, matrix products, prefill_attention(): jnp.einsum('hqk,khd->qhd', new_probs, new_values, preferred_element_type=...  8.27 us
  transfers between devices with their start and end apart: 4, of which 4 were waited for; matrix products, arithmetic and copies ran while one was open for 24% of the time, Pallas kernels for 0%

profile of v1, /device:TPU:0, one launch (start us, length us, event | category | flops | bytes accessed | tf_op | source)
XLA Modules:
  0.0 294.0 jit_solution(7164739672589543817)
XLA Ops:
  7.2 0.9 subtract_convert_fusion.2
  8.1 0.7 iota_compare_fusion.1
  8.9 0.7 dynamic_slice.6
  9.7 0.8 slice_convert_fusion.1
  10.6 40.2 %all-reduce.8 = bf16[16,2048]{1,0:T(8,128)(2,1)S(1)} all-reduce(f32[16,2048]{1,0:T(8,128)S(1)} %select_select_fusion.1), channel_id=3, replica_groups=mesh['dp'=8,'tensor'=4] {'dp'}, use_global_device_ids=true, to_apply=%region_7.8.clone | all-reduce | flops 32768 | bytes 196608
  50.8 1.2 dynamic-slice
  53.0 0.7 convert_element_type.110
  53.7 0.7 convert_element_type.111
  55.1 3.7 %fusion.9 = bf16[2,1536]{1,0:T(2,128)(2,1)S(1)} fusion(bf16[2048,1536]{1,0:T(8,128)(2,1)} %param.19, bf16[2,2048]{1,0:T(2,128)(2,1)S(1)} %get-tuple-element.7, f32[2]{0:T(128)S(1)} %add_rsqrt_fusion.1, f32[2]{0:T(128)S(1)} %broadcast_multiply_fusion.1, f32[2048]{0:T(1024)S(1)} %convert_element_type.111, f32[2048]{0:T(1024)S(1)} %convert_element_type.110, ...), kind=kOutput, calls=%fused_computation.23 | convolution fusion | flops 12613632 | bytes 6328336 | tf_op jit(solution)/shard_map/dot_general | solution.py:156
  58.9 6.3 %copy.60 = bf16[2,2048,512]{1,2,0:T(8,128)(2,1)} copy(bf16[2,2048,512]{2,1,0:T(8,128)(2,1)} %param.25) | data formatting | bytes 8388608 | tf_op jit(solution)/shard_map/reshape | solution.py:165
  65.2 2.8 fusion.34
  68.6 2.8 fusion.4
  72.1 0.7 select_select_fusion
  73.6 1.5 fusion.13
  75.8 2.1 reshape_squeeze.6
  78.0 2.3 copy.59
  80.2 1.4 iota_compare_fusion
  81.6 3.6 %subtract_convert_fusion = (f32[1024,1024]{0,1:T(8,128)}, f32[1024,1024]{0,1:T(8,128)}) fusion(s32[1024]{0:T(1024)S(1)} %iota_add_fusion), kind=kLoop, calls=%fused_computation.14 | loop fusion | flops 4194304 | bytes 8392704 | tf_op jit(solution)/shard_map/convert_element_type | solution.py:37
  85.2 16.5 %all-reduce.5.cloned.1.call-done = f32[16,2048]{1,0:T(8,128)} async-done(((f32[16,2048]{1,0:T(8,128)}), f32[16,2048]{1,0:T(8,128)}) %all-reduce.5.cloned.1.call-update) | async-done | bytes 131088 | tf_op jit(solution)/shard_map/psum | solution.py:175
  101.9 35.9 %all-gather.2.cloned.1.call-done = bf16[1024,2048]{1,0:T(8,128)(2,1)} async-done(((bf16[256,2048]{1,0:T(8,128)(2,1)}), bf16[1024,2048]{1,0:T(8,128)(2,1)}) %all-gather.2.cloned.1.call-update) | async-done | bytes 4194320 | tf_op jit(solution)/shard_map/all_gather | solution.py:120
  137.8 11.2 %add_convert_fusion = bf16[1024,1536]{1,0:T(8,128)(2,1)} fusion(bf16[1024,2048]{1,0:T(8,128)(2,1)} %all-gather.2.cloned.1.call-done, bf16[2048,1536]{1,0:T(8,128)(2,1)} %param.19, f32[1536]{0:T(1024)S(1)} %convert_element_type.113), kind=kOutput, calls=%fused_computation.10 | convolution fusion | flops 6445596672 | bytes 13637632 | tf_op jit(solution)/shard_map/dot_general | solution.py:119
  149.0 4.7 %copy.40 = bf16[1024,1536]{0,1:T(8,128)(2,1)} copy(bf16[1024,1536]{1,0:T(8,128)(2,1)} %add_convert_fusion) | data formatting | bytes 6291456 | tf_op jit(solution)/shard_map/convert_element_type | solution.py:124
  153.7 10.9 %fusion.47 = (f32[4,1024]{1,0:T(4,128)S(1)}, f32[4,1024,1024]{1,2,0:T(8,128)}) fusion(f32[1024,1024]{0,1:T(8,128)} %get-tuple-element.15, f32[4]{0:T(128)S(1)} %multiply_exponential_fusion, bf16[1024,4,3,128]{0,3,2,1:T(8,128)(2,1)} %bitcast.87, pred[1024,1024]{0,1:T(8,128)(4,1)} %iota_compare_fusion), kind=kOutput, calls=%fused_computation.96 | convolution fusion | flops 1094709248 | bytes 24133648 | tf_op jit(solution)/shard_map/qhd,khd->hqk/dot_general | solution.py:44
  164.7 4.6 %fusion.46 = (f32[4,1024]{1,0:T(4,128)S(1)}, f32[4,1024,1024]{1,2,0:T(8,128)S(1)}) fusion(f32[1024,1024]{0,1:T(8,128)S(1)} %copy-done.1, f32[4]{0:T(128)S(1)} %multiply_exponential_fusion, bf16[1024,4,3,128]{0,3,2,1:T(8,128)(2,1)S(1)} %bitcast.88, bf16[1024,4,128]{2,1,0:T(4,128)(2,1)} %reshape_squeeze.6, pred[1024]{0:T(1024)(128)(4,1)S(1)} %iota_compare_fusion.2), kind=kOutput, calls=%fused_computation.95 | convolution fusion | flops 1094709248 | bytes 23086592 | tf_op jit(solution)/shard_map/qhd,khd->hqk/dot_general | solution.py:39
  169.3 8.4 %fusion.1 = (f32[4,1024]{1,0:T(4,128)S(1)}, f32[4,1024]{1,0:T(4,128)S(1)}) fusion(f32[4,1024,1024]{1,2,0:T(8,128)} %get-tuple-element.26, f32[4,1024]{1,0:T(4,128)S(1)} %max.12, f32[4,1024,1024]{1,2,0:T(8,128)S(1)} %get-tuple-element.24), kind=kLoop, calls=%fused_computation.7 | loop fusion | flops 16769024 | bytes 33603584 | tf_op jit(solution)/shard_map/reduce_sum | solution.py:57
  177.8 4.3 %fusion.2 = f32[4,1024,128]{1,2,0:T(8,128)} fusion(bf16[1024,4,128]{0,2,1:T(8,128)(2,1)S(1)} %bitcast.90, f32[4,1024,1024]{1,2,0:T(8,128)S(1)} %get-tuple-element.24, f32[4,1024]{1,0:T(4,128)S(1)} %add.160, f32[4,1024]{1,0:T(4,128)S(1)} %max.12), kind=kOutput, calls=%fused_computation.8 | convolution fusion | flops 1086324736 | bytes 19955712 | tf_op jit(solution)/shard_map/hqk,khd->qhd/dot_general | solution.py:62
  182.1 8.3 %fusion.15 = bf16[1024,4,128]{0,2,1:T(8,128)(2,1)S(1)} fusion(f32[4,1024,128]{1,2,0:T(8,128)} %fusion.2, f32[4,1024,1024]{1,2,0:T(8,128)} %get-tuple-element.26, f32[4,1024]{1,0:T(4,128)S(1)} %add.160, f32[4,1024]{1,0:T(4,128)S(1)} %max.12, bf16[1024,4,3,128]{0,3,2,1:T(8,128)(2,1)S(1)} %bitcast.89), kind=kOutput, calls=%fused_computation.30 | convolution fusion | flops 1087373312 | bytes 21004288 | tf_op jit(solution)/shard_map/hqk,khd->qhd/dot_general | solution.py:65
  190.4 5.6 %fusion.48 = f32[1024,2048]{1,0:T(8,128)} fusion(bf16[1024,512]{0,1:T(8,128)(2,1)S(1)} %bitcast.97, bf16[512,2048]{1,0:T(8,128)(2,1)S(1)} %copy-done), kind=kOutput, calls=%fused_computation.97 | convolution fusion | flops 2147483648 | bytes 11534336 | tf_op jit(solution)/shard_map/dot_general | solution.py:136
  196.7 14.5 %all-reduce.7.cloned.1.call-done = f32[16,2048]{1,0:T(8,128)} async-done(((f32[16,2048]{1,0:T(8,128)}), f32[16,2048]{1,0:T(8,128)}) %all-reduce.7.cloned.1.call-update) | async-done | bytes 131088 | tf_op jit(solution)/shard_map/psum | solution.py:175
  211.2 1.5 add_convert_fusion.1
  212.6 72.0 %reduce-scatter.2.cloned.1.call-done = f32[256,2048]{1,0:T(8,128)} async-done(((f32[1024,2048]{1,0:T(8,128)}), f32[256,2048]{1,0:T(8,128)}) %reduce-scatter.2.cloned.1.call-update) | async-done | bytes 2097168 | tf_op jit(solution)/shard_map/reduce_scatter | solution.py:135
  284.6 2.9 fusion.14
  (56 shorter events, 4.2 us)
Async XLA Ops:
  7.2 64.4 %copy-start = (bf16[512,2048]{1,0:T(8,128)(2,1)S(1)}, bf16[512,2048]{1,0:T(8,128)(2,1)}, u32[]{:S(2)}) copy-start(bf16[512,2048]{1,0:T(8,128)(2,1)} %param.21) | copy-start | bytes 6291460
  7.2 94.5 %all-reduce.5.cloned.1.call-start = ((), (), s32[]{:S(2)}) async-start(), calls=%async_computation.3 | async-start | bytes 262144 | tf_op jit(solution)/shard_map/psum | solution.py:175
  68.0 4.0 %copy-start.7 = (s32[16]{0:T(128)S(1)}, s32[16]{0:T(128)}, u32[]{:S(2)}) copy-start(s32[16]{0:T(128)} %param.29) | copy-start | bytes 196
  68.0 4.9 %copy-start.2 = (bf16[256,2048]{1,0:T(8,128)(2,1)S(1)}, bf16[256,2048]{1,0:T(8,128)(2,1)}, u32[]{:S(2)}) copy-start(bf16[256,2048]{1,0:T(8,128)(2,1)} %param.15) | copy-start | bytes 3145732
  72.8 65.0 %all-gather.2.cloned.1.call-start = ((), (), s32[]{:S(2)}) async-start(), calls=%async_computation.1 | async-start | bytes 5242880 | tf_op jit(solution)/shard_map/all_gather | solution.py:120
  75.1 136.0 %all-reduce.7.cloned.1.call-start = ((), (), s32[]{:S(2)}) async-start(), calls=%async_computation.4 | async-start | bytes 262144 | tf_op jit(solution)/shard_map/psum | solution.py:175
  101.7 182.9 %reduce-scatter.2.cloned.1.call-start = ((), (), s32[]{:S(2)}) async-start(), calls=%async_computation.2 | async-start | bytes 10485760 | tf_op jit(solution)/shard_map/reduce_scatter | solution.py:135
  153.7 10.9 %copy-start.1 = (f32[1024,1024]{0,1:T(8,128)S(1)}, f32[1024,1024]{0,1:T(8,128)}, u32[]{:S(2)}) copy-start(f32[1024,1024]{0,1:T(8,128)} %get-tuple-element.16) | copy-start | bytes 12582916
  153.7 10.9 %copy-start.3 = (bf16[1024,1536]{0,1:T(8,128)(2,1)S(1)}, bf16[1024,1536]{0,1:T(8,128)(2,1)}, u32[]{:S(2)}) copy-start(bf16[1024,1536]{0,1:T(8,128)(2,1)} %copy.40) | copy-start | bytes 9437188
  169.3 8.5 %copy-start.4 = (bf16[1,1024,512]{1,2,0:T(8,128)(2,1)S(1)}, bf16[1,1024,512]{1,2,0:T(8,128)(2,1)}, u32[]{:S(2)}) copy-start(bf16[1,1024,512]{1,2,0:T(8,128)(2,1)} %copy.59) | copy-start | bytes 3145732
  196.0 0.7 copy-start.6
  196.0 15.2 %copy-start.5 = (bf16[2,2048]{1,0:T(2,128)(2,1)S(1)}, bf16[2,2048]{1,0:T(2,128)(2,1)}, u32[]{:S(2)}) copy-start(bf16[2,2048]{1,0:T(2,128)(2,1)} %param.16) | copy-start | bytes 24580
Sparse Core Ops, SparseCore 0:
  73.0 28.6 all-reduce.4
  103.3 34.4 all-gather.1
  141.5 69.5 all-reduce.6
  213.6 70.9 reduce-scatter.1
